TPU v7x, 128 devices: a whole 4x4x4 slice. The times are simulated.
128 devices in a mesh: req: 16 (over z, x), exp: 8 (over y, core).
Axes of the slice: x: 4, y: 4, z: 4, core: 2. Of those that a mesh axis runs over, the one named last changes fastest.
Arguments:
- tokens: bfloat16 [12288, 2880], P(('req', 'exp')), may hold values from -6 to 6
- attn_gain: float32 [2880], replicated, may hold values from 0.5 to 8
- w_query: bfloat16 [2880, 4096], P(None, 'exp'), may hold values from -0.109375 to 0.109375
- key_weight: bfloat16 [2880, 512], P(None, 'exp'), may hold values from -0.109375 to 0.109375
- value_weight: bfloat16 [2880, 512], P(None, 'exp'), may hold values from -0.109375 to 0.109375
- sinks: float32 [64], P('exp'), may hold values from -1 to 3
- w_out: bfloat16 [4096, 2880], P('exp'), may hold values from -0.09375 to 0.09375
- ffn_gain: float32 [2880], replicated, may hold values from 0.25 to 1.75
- router: bfloat16 [2880, 32], replicated, may hold values from -0.109375 to 0.109375
- routes: int32 [12288, 4], P(('req', 'exp')), may hold values from 0 to 31, all different within a row; in each aligned block of 96 rows (0 to 95, 96 to 191, ...) at most 14 rows name the same one
- lengths: int32 [16, 6], P('req'), may hold values from 1 to 384, 768 in all within a row
- expert_gate: bfloat16 [128, 2880, 720], P(('req', 'exp')), may hold values from -0.109375 to 0.109375
- expert_up: bfloat16 [128, 2880, 720], P(('req', 'exp')), may hold values from -0.109375 to 0.109375
- expert_down: bfloat16 [128, 720, 2880], P(('req', 'exp')), may hold values from -0.109375 to 0.109375
Outputs:
- layer_out: bfloat16 [12288, 2880], P(('req', 'exp'))
Inputs may be any that keep to these rules, and one draw needn't show every extreme that they name: `routes`: in the rows of one device no expert is named by more than 14 rows, a bound that some block reaches; a row names 4 different experts.
All inputs are finite; a program needn't handle non-finite values.
Results may differ from a plain program's by a relative error of at most 0.02.
The roundings to bfloat16 on the way count: a program that leaves them out, or rounds other values in their place, can miss the bound.
Values may be sent and summed in bfloat16 or wider, within the bound.
No kernel may reach another device: no remote copies, remote signals or barrier semaphores. Data moves between devices by JAX's collectives and lax.ppermute only.
A program may use at most 192 MiB of HBM per device.

v0:
```python
import jax
import jax.numpy as jnp
from jax import lax
from jax.sharding import PartitionSpec as P

QUERY_HEADS = 64
KEY_VALUE_HEADS = 8
HEAD_DIM = 64
EXPERTS = 32
TOPK = 4
CAP = 14


def rms_norm(value_rows, gain):
    mean_sq = jnp.mean(value_rows * value_rows, axis=-1, keepdims=True)
    return value_rows * lax.rsqrt(mean_sq + 1e-05) * gain


def rotate(value_rows, offset):
    half = value_rows.shape[-1] // 2
    freqs = jnp.exp(
        -(2.0 * jnp.arange(half, dtype=jnp.float32) / value_rows.shape[-1])
        * jnp.log(jnp.float32(150000.0))
    )
    angle = offset.astype(jnp.float32)[:, None] * freqs[None, :]
    cosine = jnp.cos(angle)[:, None, :]
    sine = jnp.sin(angle)[:, None, :]
    first = value_rows[..., :half]
    second = value_rows[..., half:]
    return jnp.concatenate(
        [first * cosine - second * sine, second * cosine + first * sine], axis=-1
    )


def per_device(
    tokens,
    attn_gain,
    w_query,
    key_weight,
    value_weight,
    sinks,
    w_out,
    ffn_gain,
    router,
    routes,
    lengths,
    expert_gate,
    expert_up,
    expert_down,
):
    tok_rows = tokens.shape[0]
    model_width = tokens.shape[1]
    local_heads = w_query.shape[1] // HEAD_DIM
    local_kv = key_weight.shape[1] // HEAD_DIM
    head_group = QUERY_HEADS // KEY_VALUE_HEADS
    normed_input = rms_norm(tokens.astype(jnp.float32), attn_gain).astype(jnp.bfloat16)
    piece = lax.all_gather(normed_input, "exp", axis=0, tiled=True)
    projected = jnp.concatenate(
        [
            jnp.dot(piece, w_query, preferred_element_type=jnp.float32),
            jnp.dot(piece, key_weight, preferred_element_type=jnp.float32),
            jnp.dot(piece, value_weight, preferred_element_type=jnp.float32),
        ],
        axis=1,
    )
    item_count = projected.shape[0]
    lens = lengths[0]
    ends = jnp.cumsum(lens)
    starts = ends - lens
    position = jnp.arange(item_count, dtype=jnp.int32)
    member = ((position[:, None] >= starts[None, :]) & (position[:, None] < ends[None, :])).astype(
        jnp.int32
    )
    segment = jnp.sum(member * jnp.arange(lens.shape[0], dtype=jnp.int32)[None, :], axis=1)
    offset = position - jnp.sum(member * starts[None, :], axis=1)
    q_width = local_heads * HEAD_DIM
    kv_width = local_kv * HEAD_DIM
    query_rows = rotate(
        projected[:, :q_width].reshape(item_count, local_heads, HEAD_DIM), offset
    ).astype(jnp.bfloat16)
    key_rows = rotate(
        projected[:, q_width : q_width + kv_width].reshape(item_count, local_kv, HEAD_DIM), offset
    ).astype(jnp.bfloat16)
    value_rows = (
        projected[:, q_width + kv_width :]
        .reshape(item_count, local_kv, HEAD_DIM)
        .astype(jnp.bfloat16)
    )
    grouped_heads = query_rows.reshape(item_count, local_kv, head_group, HEAD_DIM)
    scores = jnp.einsum(
        "qcgd,kcd->cgqk", grouped_heads, key_rows, preferred_element_type=jnp.float32
    ) * HEAD_DIM ** (-0.5)
    allowed = (segment[:, None] == segment[None, :]) & (position[None, :] <= position[:, None])
    sink_score_logit = sinks.reshape(local_kv, head_group, 1, 1)
    masked = jnp.where(allowed[None, None], scores, -jnp.inf)
    top = jnp.maximum(jnp.max(masked, axis=-1, keepdims=True), sink_score_logit)
    expo = jnp.where(allowed[None, None], jnp.exp(scores - top), 0.0)
    denom = jnp.sum(expo, axis=-1, keepdims=True) + jnp.exp(sink_score_logit - top)
    probs = (expo / denom).astype(jnp.bfloat16)
    attended = jnp.einsum("cgqk,kcd->qcgd", probs, value_rows, preferred_element_type=jnp.float32)
    attended = attended.reshape(item_count, q_width).astype(jnp.bfloat16)
    attn_sum = lax.psum_scatter(
        jnp.dot(attended, w_out, preferred_element_type=jnp.float32).astype(jnp.bfloat16),
        "exp",
        scatter_dimension=0,
        tiled=True,
    ).astype(jnp.float32)
    residual = (tokens.astype(jnp.float32) + attn_sum).astype(jnp.bfloat16)
    normed2 = rms_norm(residual.astype(jnp.float32), ffn_gain).astype(jnp.bfloat16)
    logits = jnp.dot(normed2, router, preferred_element_type=jnp.float32)
    picked = jnp.take_along_axis(logits, routes, axis=1)
    weights = jax.nn.softmax(picked, axis=-1)
    flat_routes = routes.reshape(-1)
    expert_ids = jnp.arange(EXPERTS, dtype=jnp.int32)
    onehot_route = (flat_routes[:, None] == expert_ids[None, :]).astype(jnp.int32)
    rank = jnp.cumsum(onehot_route, axis=0) - 1
    slot_rank = jnp.sum(onehot_route * rank, axis=1)
    flat_slot = flat_routes * CAP + slot_rank
    slot_ids = jnp.arange(EXPERTS * CAP, dtype=jnp.int32)
    dispatch_table = (slot_ids[:, None] == flat_slot[None, :]).astype(jnp.bfloat16)
    repeated = jnp.repeat(normed2, TOPK, axis=0)
    packed = jnp.dot(dispatch_table, repeated, preferred_element_type=jnp.float32).astype(
        jnp.bfloat16
    )
    n_req = lax.axis_size("req")
    n_exp = lax.axis_size("exp")
    devices = n_req * n_exp
    split = devices // EXPERTS
    send_rows = jnp.broadcast_to(
        packed.reshape(EXPERTS, 1, CAP, model_width), (EXPERTS, split, CAP, model_width)
    ).reshape(devices, CAP, model_width)
    received = lax.all_to_all(send_rows, ("req", "exp"), split_axis=0, concat_axis=0, tiled=True)
    flat_rows = received.reshape(-1, model_width)
    gate = jnp.dot(flat_rows, expert_gate[0], preferred_element_type=jnp.float32)
    up_val = jnp.dot(flat_rows, expert_up[0], preferred_element_type=jnp.float32)
    hidden = ((up_val + 1.0) * gate * jax.nn.sigmoid(1.702 * gate)).astype(jnp.bfloat16)
    slice_out = jnp.dot(hidden, expert_down[0], preferred_element_type=jnp.float32).astype(
        jnp.bfloat16
    )
    returned = lax.all_to_all(
        slice_out.reshape(received.shape), ("req", "exp"), split_axis=0, concat_axis=0, tiled=True
    )
    summed = returned.astype(jnp.float32).reshape(EXPERTS, split, CAP, model_width).sum(axis=1)
    summed = summed.reshape(EXPERTS * CAP, model_width)
    picked_rows = jnp.take(summed, flat_slot, axis=0).reshape(tok_rows, TOPK, model_width)
    moe_sum = jnp.sum(weights[:, :, None] * picked_rows, axis=1)
    return (residual.astype(jnp.float32) + moe_sum).astype(jnp.bfloat16)


def solution(mesh):
    return jax.shard_map(
        per_device,
        mesh=mesh,
        in_specs=(
            P(("req", "exp"), None),
            P(),
            P(None, "exp"),
            P(None, "exp"),
            P(None, "exp"),
            P("exp"),
            P("exp", None),
            P(),
            P(),
            P(("req", "exp"), None),
            P("req", None),
            P(("req", "exp"), None, None),
            P(("req", "exp"), None, None),
            P(("req", "exp"), None, None),
        ),
        out_specs=P(("req", "exp"), None),
        check_vma=False,
    )
```

profile of v0, /device:TPU:14, one launch (start us, length us, event | category | flops | bytes accessed | tf_op | source)
XLA Modules:
  0.0 587.9 jit_solution(4064006883043466249)
XLA Ops:
  13.2 31.8 %all-gather.2.cloned.1.call-done = bf16[768,2880]{1,0:T(8,128)(2,1)} async-done(((bf16[96,2880]{1,0:T(8,128)(2,1)}), bf16[768,2880]{1,0:T(8,128)(2,1)}) %all-gather.2.cloned.1.call-update) | async-done | bytes 4423696 | tf_op jit(solution)/shard_map/all_gather | solution.py:57
  45.0 3.9 convolution_bitcast_fusion
  49.4 4.6 fusion.59
  54.2 8.6 %fusion = (f32[8,768]{1,0:T(8,128)S(1)}, f32[768,768,8]{1,0,2:T(8,128)}) fusion(pred[768,768]{0,1:T(8,128)(4,1)S(1)} %fusion.13, bf16[768,8,32]{0,2,1:T(8,128)(2,1)S(1)} %get-tuple-element.10, bf16[768,8,32]{0,2,1:T(8,128)(2,1)S(1)} %get-tuple-element.9, bf16[768,32]{0,1:T(8,128)(2,1)S(1)} %get-tuple-element.12, bf16[768,32]{0,1:T(8,128)(2,1)S(1)} %get-tuple-element.11), kind=kOutput, calls=%fused_computation.5 | convolution fusion | flops 619898880 | bytes 20373504 | tf_op jit(solution)/shard_map/qcgd,kcd->cgqk/dot_general | solution.py:90
  64.2 10.8 %fusion.3 = f32[8,768]{1,0:T(8,128)} fusion(f32[768,768,8]{1,0,2:T(8,128)} %get-tuple-element.16, f32[8,768]{1,0:T(8,128)} %broadcast_maximum_fusion, pred[768,768]{0,1:T(8,128)(4,1)S(1)} %fusion.13), kind=kLoop, calls=%fused_computation.9 | loop fusion | flops 18868224 | bytes 19513344 | tf_op jit(solution)/shard_map/reduce_sum | solution.py:98
  76.4 14.1 %fusion.16 = bf16[64,8,768]{2,0,1:T(8,128)(2,1)} fusion(f32[8,768]{1,0:T(8,128)} %exponential_add_fusion, f32[8,768]{1,0:T(8,128)} %broadcast_maximum_fusion, f32[768,768,8]{1,0,2:T(8,128)} %get-tuple-element.16, pred[768,768]{0,1:T(8,128)(4,1)S(1)} %fusion.13, bf16[768,2880]{1,0:T(8,128)(2,1)} %all-gather.2.cloned.1.call-done, bf16[2880,64]{0,1:T(8,128)(2,1)} %param.18), kind=kOutput, calls=%fused_computation.30 | convolution fusion | flops 911130624 | bytes 25092096 | tf_op jit(solution)/shard_map/cgqk,kcd->qcgd/dot_general | solution.py:100
  90.5 5.8 convolution_convert_fusion.1
  98.7 33.6 %reduce-scatter.2.cloned.1.call-done = bf16[96,2880]{1,0:T(8,128)(2,1)} async-done(((bf16[768,2880]{1,0:T(8,128)(2,1)}), bf16[96,2880]{1,0:T(8,128)(2,1)}) %reduce-scatter.2.cloned.1.call-update) | async-done | bytes 552976 | tf_op jit(solution)/shard_map/reduce_scatter | solution.py:102
  138.1 4.7 convolution_convert_fusion.2
  142.8 4.4 broadcast_in_dim.41
  147.2 7.1 %broadcast_in_dim.42 = bf16[32,4,14,2880]{3,2,1,0:T(8,128)(2,1)} broadcast(bf16[32,14,2880]{2,1,0:T(8,128)(2,1)} %broadcast_in_dim.41), dimensions={0,2,3} | broadcast | bytes 12902400 | tf_op jit(solution)/shard_map/broadcast_in_dim | solution.py:129
  154.3 146.0 %all_to_all.10 = bf16[128,14,2880]{2,1,0:T(8,128)(2,1)} all-to-all(bf16[128,14,2880]{2,1,0:T(8,128)(2,1)} %bitcast.104), channel_id=1, replica_groups=mesh['req'=16,'exp'=8] {'req','exp'}, dimensions={0} | all-to-all | bytes 20643840 | tf_op jit(solution)/shard_map/all_to_all | solution.py:132
  300.4 15.4 %reshape.419 = bf16[1792,2880]{1,0:T(8,128)(2,1)} reshape(bf16[128,14,2880]{2,1,0:T(8,128)(2,1)} %all_to_all.10) | data formatting | bytes 20643840 | tf_op jit(solution)/shard_map/reshape | solution.py:133
  315.7 14.6 %fusion.7 = f32[1792,720]{0,1:T(8,128)} fusion(bf16[1792,2880]{1,0:T(8,128)(2,1)} %reshape.419, bf16[1,2880,720]{1,2,0:T(8,128)(2,1)} %param.25), kind=kOutput, calls=%fused_computation.18 | convolution fusion | flops 7431782400 | bytes 19630080 | tf_op jit(solution)/shard_map/dot_general | solution.py:134
  330.3 27.2 %convolution_convert_fusion = bf16[1792,2880]{0,1:T(8,128)(2,1)} fusion(bf16[1,720,2880]{2,1,0:T(8,128)(2,1)} %param.27, f32[1792,720]{0,1:T(8,128)} %fusion.7, bf16[1792,2880]{1,0:T(8,128)(2,1)} %reshape.419, bf16[1,2880,720]{1,2,0:T(8,128)(2,1)} %param.26), kind=kOutput, calls=%fused_computation.10 | convolution fusion | flops 14879047680 | bytes 34099200 | tf_op jit(solution)/shard_map/dot_general | solution.py:137
  357.6 14.3 %copy.49 = bf16[1792,2880]{1,0:T(8,128)(2,1)} copy(bf16[1792,2880]{0,1:T(8,128)(2,1)} %convolution_convert_fusion) | data formatting | bytes 20643840 | tf_op jit(solution)/shard_map/convert_element_type | solution.py:137
  371.9 14.4 %reshape.420 = bf16[128,14,2880]{2,1,0:T(8,128)(2,1)} reshape(bf16[1792,2880]{1,0:T(8,128)(2,1)} %copy.49) | data formatting | bytes 20643840 | tf_op jit(solution)/shard_map/reshape | solution.py:141
  386.3 8.2 %all-to-all-start.1 = ((bf16[128,14,2880]{2,1,0:T(8,128)(2,1)}), bf16[128,14,2880]{2,1,0:T(8,128)(2,1)}, u32[]{:S(2)}, u32[]{:S(2)}) async-start(bf16[128,14,2880]{2,1,0:T(8,128)(2,1)} %reshape.420), calls=%async_computation.2 | async-start | bytes 24117248 | tf_op jit(solution)/shard_map/all_to_all | solution.py:140
  399.5 143.8 %all-to-all-done.1 = bf16[128,14,2880]{2,1,0:T(8,128)(2,1)} async-done(((bf16[128,14,2880]{2,1,0:T(8,128)(2,1)}), bf16[128,14,2880]{2,1,0:T(8,128)(2,1)}, u32[]{:S(2)}, u32[]{:S(2)}) %all-to-all-start.1) | async-done | bytes 10321952 | tf_op jit(solution)/shard_map/all_to_all | solution.py:140
  543.3 9.8 %convert_reduce_fusion = f32[32,14,2880]{2,1,0:T(8,128)} fusion(bf16[128,14,2880]{2,1,0:T(8,128)(2,1)} %all-to-all-done.1), kind=kLoop, calls=%fused_computation.2 | loop fusion | flops 9031680 | bytes 15482880 | tf_op jit(solution)/shard_map/reduce_sum | solution.py:143
  553.1 5.6 reshape.423
  558.7 9.1 %gather_fusion = f32[384,2880]{1,0:T(8,128)} fusion(f32[448,2880]{1,0:T(8,128)} %reshape.423, s32[1024]{0:T(1024)S(1)} %pad_clamp_fusion), kind=kCustom, calls=%fused_computation | custom fusion | bytes 8848896 | tf_op jit(solution)/shard_map/jit(_take)/gather | solution.py:145
  567.8 5.5 gather.12
  573.3 6.5 %multiply_reduce_fusion = f32[96,2880]{1,0:T(8,128)S(1)} fusion(f32[96,4,2880]{2,1,0:T(4,128)} %gather.12, f32[96,4]{1,0:T(8,128)} %copy.43, pred[96,4]{1,0:T(8,128)(4,1)S(1)} %copy.48), kind=kLoop, calls=%fused_computation.15 | loop fusion | flops 3041280 | bytes 5531520 | tf_op jit(solution)/shard_map/reduce_sum | solution.py:146
  (77 shorter events, 24.0 us)
Async XLA Ops:
  6.5 83.9 %copy-start = (bf16[512,2880]{0,1:T(8,128)(2,1)S(1)}, bf16[512,2880]{0,1:T(8,128)(2,1)}, u32[]{:S(2)}) copy-start(bf16[512,2880]{0,1:T(8,128)(2,1)} %param.20) | copy-start | bytes 8847364
  6.5 38.4 %all-gather.2.cloned.1.call-start = ((), (), s32[]{:S(2)}) async-start(), calls=%async_computation.3 | async-start | bytes 5087232 | tf_op jit(solution)/shard_map/all_gather | solution.py:57
  10.1 122.3 %reduce-scatter.2.cloned.1.call-start = ((), (), s32[]{:S(2)}) async-start(), calls=%async_computation.4 | async-start | bytes 5087232 | tf_op jit(solution)/shard_map/reduce_scatter | solution.py:102
  45.0 4.4 copy-start.4
  49.3 4.7 copy-start.5
  49.3 4.7 copy-start.6
  54.2 9.3 %copy-start.11 = (f32[8]{0:T(128)S(1)}, f32[8]{0:T(128)}, u32[]{:S(2)}) copy-start(f32[8]{0:T(128)} %param.19) | copy-start | bytes 100
  62.9 0.6 copy-start.7
  96.3 0.7 copy-start.9
  96.3 36.1 %copy-start.2 = (bf16[96,2880]{1,0:T(8,128)(2,1)S(1)}, bf16[96,2880]{1,0:T(8,128)(2,1)}, u32[]{:S(2)}) copy-start(bf16[96,2880]{1,0:T(8,128)(2,1)} %param.14) | copy-start | bytes 1658884
  96.3 37.4 %copy-start.10 = (f32[2880]{0:T(1024)S(1)}, f32[2880]{0:T(1024)}, u32[]{:S(2)}) copy-start(f32[2880]{0:T(1024)} %param.21) | copy-start | bytes 34564
  386.3 9.0 %copy-start.8 = (bf16[2880,32]{0,1:T(8,128)(2,1)S(1)}, bf16[2880,32]{0,1:T(8,128)(2,1)}, u32[]{:S(2)}) copy-start(bf16[2880,32]{0,1:T(8,128)(2,1)} %param.22) | copy-start | bytes 552964
  386.3 157.0 %all-to-all-start.1 = ((bf16[128,14,2880]{2,1,0:T(8,128)(2,1)}), bf16[128,14,2880]{2,1,0:T(8,128)(2,1)}, u32[]{:S(2)}, u32[]{:S(2)}) async-start(bf16[128,14,2880]{2,1,0:T(8,128)(2,1)} %reshape.420), calls=%async_computation.2 | async-start | bytes 24117248 | tf_op jit(solution)/shard_map/all_to_all | solution.py:140
  567.8 13.1 %copy-start.1 = (bf16[512,2880]{0,1:T(8,128)(2,1)S(1)}, bf16[512,2880]{0,1:T(8,128)(2,1)}, u32[]{:S(2)}) copy-start(bf16[512,2880]{0,1:T(8,128)(2,1)} %param.20) | copy-start | bytes 8847364
  573.3 6.5 %copy-start.3 = (bf16[96,2880]{1,0:T(8,128)(2,1)S(1)}, bf16[96,2880]{1,0:T(8,128)(2,1)}, u32[]{:S(2)}) copy-start(bf16[96,2880]{1,0:T(8,128)(2,1)} %reduce-scatter.2.cloned.1.call-done) | copy-start | bytes 1658884
Sparse Core Ops, SparseCore 0:
  10.2 34.7 all-gather.1
  96.5 35.8 reduce-scatter.1
where the time goes:
time: 594 us; the launch traced here: 588 us
  waiting for transfers between devices  209 us (35%)
  blocking collectives  146 us (25%)
  local copies, waits for them, and re-layouts  85.3 us (14%)
  matrix products  83.9 us (14%)
  other arithmetic  41.3 us (7%)
  between operations  13.9 us (2%)
  starting transfers between devices  8.24 us (1%)
    all_to_all x1, blocking collectives, per_device(): lax.all_to_all(send_rows, ('req', 'exp'), split_axis=0, concat_axis=0, ti...  146 us
    all_to_all x1, waiting for transfers between devices, per_device(): lax.all_to_all(slice_out.reshape(received.shape), ('req', 'exp'), split_a...  144 us
    reduce_scatter x1, waiting for transfers between devices, per_device(): lax.psum_scatter(jnp.dot(attended, w_out, preferred_element_type=jnp.floa...  33.6 us
    all_gather x1, waiting for transfers between devices, per_device(): piece = lax.all_gather(normed_input, 'exp', axis=0, tiled=True)  31.8 us
    dot_general x1, matrix products, per_device(): jnp.dot(hidden, expert_down[0], preferred_element_type=jnp.float32)  27.2 us
    reshape x1, local copies, waits for them, and re-layouts, per_device(): flat_rows = received.reshape(-1, model_width)  15.4 us
    gather x2, local copies, waits for them, and re-layouts, per_device(): jnp.take(summed, flat_slot, axis=0).reshape(tok_rows, TOPK, model_width)  14.6 us
    dot_general x1, matrix products, per_device(): jnp.dot(flat_rows, expert_gate[0], preferred_element_type=jnp.float32)  14.6 us
  transfers between devices with their start and end apart: 3, of which 3 were waited for; matrix products, arithmetic and copies ran while one was open for 2% of the time, Pallas kernels for 0%

commit v1 on v0

--- a/solution.py
+++ b/solution.py
@@ -54,7 +54,10 @@
     local_kv = key_weight.shape[1] // HEAD_DIM
     head_group = QUERY_HEADS // KEY_VALUE_HEADS
     normed_input = rms_norm(tokens.astype(jnp.float32), attn_gain).astype(jnp.bfloat16)
-    piece = lax.all_gather(normed_input, "exp", axis=0, tiled=True)
+    n_dev = lax.axis_size("exp")
+    blocks = jnp.stack([normed_input for _ in range(n_dev)])
+    blocks = lax.all_to_all(blocks, "exp", split_axis=0, concat_axis=0)
+    piece = jnp.concatenate(blocks, axis=0)
     projected = jnp.concatenate(
         [
             jnp.dot(piece, w_query, preferred_element_type=jnp.float32),

time: 594 us -> 622 us (1.047)
  waiting for transfers between devices: 209 us -> 223 us
  local copies, waits for them, and re-layouts: 85.3 us -> 92.3 us
    all_to_all x0 -> x1, waiting for transfers between devices: none -> 45.5 us  [per_device(): blocks = lax.all_to_all(blocks, 'exp', split_axis=0, concat_axis=0)]
    all_gather x1 -> x0, waiting for transfers between devices: 31.8 us -> none  [per_device(): piece = lax.all_gather(normed_input, 'exp', axis=0, tiled=True)]
where the time goes in v1:
time: 622 us; the launch traced here: 612 us
  waiting for transfers between devices  223 us (36%)
  blocking collectives  146 us (23%)
  local copies, waits for them, and re-layouts  92.3 us (15%)
  matrix products  84.2 us (14%)
  other arithmetic  39 us (6%)
  between operations  13.9 us (2%)
  starting transfers between devices  13.1 us (2%)
    all_to_all x1, blocking collectives, per_device(): lax.all_to_all(send_rows, ('req', 'exp'), split_axis=0, concat_axis=0, ti...  146 us
    all_to_all x1, waiting for transfers between devices, per_device(): lax.all_to_all(slice_out.reshape(received.shape), ('req', 'exp'), split_a...  144 us
    all_to_all x1, waiting for transfers between devices, per_device(): blocks = lax.all_to_all(blocks, 'exp', split_axis=0, concat_axis=0)  45.5 us
    reduce_scatter x1, waiting for transfers between devices, per_device(): lax.psum_scatter(jnp.dot(attended, w_out, preferred_element_type=jnp.floa...  34.2 us
    dot_general x1, matrix products, per_device(): jnp.dot(hidden, expert_down[0], preferred_element_type=jnp.float32)  27.2 us
    reshape x1, local copies, waits for them, and re-layouts, per_device(): flat_rows = received.reshape(-1, model_width)  15.4 us
    gather x2, local copies, waits for them, and re-layouts, per_device(): jnp.take(summed, flat_slot, axis=0).reshape(tok_rows, TOPK, model_width)  14.6 us
    dot_general x1, matrix products, per_device(): jnp.dot(flat_rows, expert_gate[0], preferred_element_type=jnp.float32)  14.6 us
  transfers between devices with their start and end apart: 3, of which 3 were waited for; matrix products, arithmetic and copies ran while one was open for 2% of the time, Pallas kernels for 0%

profile of v1, /device:TPU:14, one launch (start us, length us, event | category | flops | bytes accessed | tf_op | source)
XLA Modules:
  0.0 612.2 jit_solution(966165134406298358)
XLA Ops:
  11.6 4.9 all-to-all-start
  16.5 4.6 copy.46
  22.9 45.5 %all-to-all-done = bf16[8,96,2880]{2,1,0:T(8,128)(2,1)} async-done(((bf16[8,96,2880]{2,1,0:T(8,128)(2,1)}), bf16[8,96,2880]{2,1,0:T(8,128)(2,1)}, u32[]{:S(2)}, u32[]{:S(2)}) %all-to-all-start) | async-done | bytes 4423712 | tf_op jit(solution)/shard_map/all_to_all | solution.py:59
  72.8 5.0 fusion.59
  78.0 8.2 %fusion = (f32[8,768]{1,0:T(8,128)S(1)}, f32[768,768,8]{1,0,2:T(8,128)}) fusion(pred[768,768]{0,1:T(8,128)(4,1)S(1)} %fusion.13, bf16[768,8,32]{0,2,1:T(8,128)(2,1)S(1)} %get-tuple-element.10, bf16[768,8,32]{0,2,1:T(8,128)(2,1)S(1)} %get-tuple-element.9, bf16[768,32]{0,1:T(8,128)(2,1)S(1)} %get-tuple-element.12, bf16[768,32]{0,1:T(8,128)(2,1)S(1)} %get-tuple-element.11), kind=kOutput, calls=%fused_computation.5 | convolution fusion | flops 619898880 | bytes 20373504 | tf_op jit(solution)/shard_map/qcgd,kcd->cgqk/dot_general | solution.py:93
  87.4 10.8 %fusion.3 = f32[8,768]{1,0:T(8,128)} fusion(f32[768,768,8]{1,0,2:T(8,128)} %get-tuple-element.16, f32[8,768]{1,0:T(8,128)} %broadcast_maximum_fusion, pred[768,768]{0,1:T(8,128)(4,1)S(1)} %fusion.13), kind=kLoop, calls=%fused_computation.9 | loop fusion | flops 18868224 | bytes 19513344 | tf_op jit(solution)/shard_map/reduce_sum | solution.py:101
  99.7 14.5 %fusion.16 = bf16[64,8,768]{2,0,1:T(8,128)(2,1)} fusion(f32[8,768]{1,0:T(8,128)} %exponential_add_fusion, f32[8,768]{1,0:T(8,128)} %broadcast_maximum_fusion, f32[768,768,8]{1,0,2:T(8,128)} %get-tuple-element.16, pred[768,768]{0,1:T(8,128)(4,1)S(1)} %fusion.13, bf16[768,2880]{1,0:T(8,128)(2,1)} %bitcast, bf16[2880,64]{0,1:T(8,128)(2,1)} %param.18), kind=kOutput, calls=%fused_computation.30 | convolution fusion | flops 911130624 | bytes 25092096 | tf_op jit(solution)/shard_map/cgqk,kcd->qcgd/dot_general | solution.py:103
  114.2 5.8 convolution_convert_fusion.1
  122.3 34.2 %reduce-scatter.2.cloned.1.call-done = bf16[96,2880]{1,0:T(8,128)(2,1)} async-done(((bf16[768,2880]{1,0:T(8,128)(2,1)}), bf16[96,2880]{1,0:T(8,128)(2,1)}) %reduce-scatter.2.cloned.1.call-update) | async-done | bytes 552976 | tf_op jit(solution)/shard_map/reduce_scatter | solution.py:105
  162.2 4.7 convolution_convert_fusion.2
  171.3 7.1 %broadcast_in_dim.42 = bf16[32,4,14,2880]{3,2,1,0:T(8,128)(2,1)} broadcast(bf16[32,14,2880]{2,1,0:T(8,128)(2,1)} %broadcast_in_dim.41), dimensions={0,2,3} | broadcast | bytes 12902400 | tf_op jit(solution)/shard_map/broadcast_in_dim | solution.py:132
  178.4 146.2 %all_to_all.15 = bf16[128,14,2880]{2,1,0:T(8,128)(2,1)} all-to-all(bf16[128,14,2880]{2,1,0:T(8,128)(2,1)} %bitcast.109), channel_id=1, replica_groups=mesh['req'=16,'exp'=8] {'req','exp'}, dimensions={0} | all-to-all | bytes 20643840 | tf_op jit(solution)/shard_map/all_to_all | solution.py:135
  324.7 15.4 %reshape.423 = bf16[1792,2880]{1,0:T(8,128)(2,1)} reshape(bf16[128,14,2880]{2,1,0:T(8,128)(2,1)} %all_to_all.15) | data formatting | bytes 20643840 | tf_op jit(solution)/shard_map/reshape | solution.py:136
  340.0 14.6 %fusion.7 = f32[1792,720]{0,1:T(8,128)} fusion(bf16[1792,2880]{1,0:T(8,128)(2,1)} %reshape.423, bf16[1,2880,720]{1,2,0:T(8,128)(2,1)} %param.25), kind=kOutput, calls=%fused_computation.18 | convolution fusion | flops 7431782400 | bytes 19630080 | tf_op jit(solution)/shard_map/dot_general | solution.py:137
  354.6 27.2 %convolution_convert_fusion = bf16[1792,2880]{0,1:T(8,128)(2,1)} fusion(bf16[1,720,2880]{2,1,0:T(8,128)(2,1)} %param.27, f32[1792,720]{0,1:T(8,128)} %fusion.7, bf16[1792,2880]{1,0:T(8,128)(2,1)} %reshape.423, bf16[1,2880,720]{1,2,0:T(8,128)(2,1)} %param.26), kind=kOutput, calls=%fused_computation.10 | convolution fusion | flops 14879047680 | bytes 34099200 | tf_op jit(solution)/shard_map/dot_general | solution.py:140
  381.8 14.3 %copy.57 = bf16[1792,2880]{1,0:T(8,128)(2,1)} copy(bf16[1792,2880]{0,1:T(8,128)(2,1)} %convolution_convert_fusion) | data formatting | bytes 20643840 | tf_op jit(solution)/shard_map/convert_element_type | solution.py:140
  396.2 14.4 %reshape.424 = bf16[128,14,2880]{2,1,0:T(8,128)(2,1)} reshape(bf16[1792,2880]{1,0:T(8,128)(2,1)} %copy.57) | data formatting | bytes 20643840 | tf_op jit(solution)/shard_map/reshape | solution.py:144
  410.6 8.2 %all-to-all-start.2 = ((bf16[128,14,2880]{2,1,0:T(8,128)(2,1)}), bf16[128,14,2880]{2,1,0:T(8,128)(2,1)}, u32[]{:S(2)}, u32[]{:S(2)}) async-start(bf16[128,14,2880]{2,1,0:T(8,128)(2,1)} %reshape.424), calls=%async_computation.3 | async-start | bytes 24117248 | tf_op jit(solution)/shard_map/all_to_all | solution.py:143
  423.8 143.8 %all-to-all-done.2 = bf16[128,14,2880]{2,1,0:T(8,128)(2,1)} async-done(((bf16[128,14,2880]{2,1,0:T(8,128)(2,1)}), bf16[128,14,2880]{2,1,0:T(8,128)(2,1)}, u32[]{:S(2)}, u32[]{:S(2)}) %all-to-all-start.2) | async-done | bytes 10321952 | tf_op jit(solution)/shard_map/all_to_all | solution.py:143
  567.6 9.8 %convert_reduce_fusion = f32[32,14,2880]{2,1,0:T(8,128)} fusion(bf16[128,14,2880]{2,1,0:T(8,128)(2,1)} %all-to-all-done.2), kind=kLoop, calls=%fused_computation.2 | loop fusion | flops 9031680 | bytes 15482880 | tf_op jit(solution)/shard_map/reduce_sum | solution.py:146
  577.4 5.6 reshape.427
  583.0 9.1 %gather_fusion = f32[384,2880]{1,0:T(8,128)} fusion(f32[448,2880]{1,0:T(8,128)} %reshape.427, s32[1024]{0:T(1024)S(1)} %pad_clamp_fusion), kind=kCustom, calls=%fused_computation | custom fusion | bytes 8848896 | tf_op jit(solution)/shard_map/jit(_take)/gather | solution.py:148
  592.1 5.5 gather.12
  597.6 6.5 %multiply_reduce_fusion = f32[96,2880]{1,0:T(8,128)S(1)} fusion(f32[96,4,2880]{2,1,0:T(4,128)} %gather.12, f32[96,4]{1,0:T(8,128)} %copy.51, pred[96,4]{1,0:T(8,128)(4,1)S(1)} %copy.56), kind=kLoop, calls=%fused_computation.15 | loop fusion | flops 3041280 | bytes 5531520 | tf_op jit(solution)/shard_map/reduce_sum | solution.py:149
  (80 shorter events, 32.4 us)
Async XLA Ops:
  6.5 107.7 %copy-start = (bf16[512,2880]{0,1:T(8,128)(2,1)S(1)}, bf16[512,2880]{0,1:T(8,128)(2,1)}, u32[]{:S(2)}) copy-start(bf16[512,2880]{0,1:T(8,128)(2,1)} %param.20) | copy-start | bytes 8847364
  11.6 56.8 %all-to-all-start = ((bf16[8,96,2880]{2,1,0:T(8,128)(2,1)}), bf16[8,96,2880]{2,1,0:T(8,128)(2,1)}, u32[]{:S(2)}, u32[]{:S(2)}) async-start(bf16[8,96,2880]{2,1,0:T(8,128)(2,1)} %stack.2), calls=%async_computation | async-start | bytes 9043968 | tf_op jit(solution)/shard_map/all_to_all | solution.py:59
  16.5 4.6 copy-start.12
  16.5 140.0 %reduce-scatter.2.cloned.1.call-start = ((), (), s32[]{:S(2)}) async-start(), calls=%async_computation.4 | async-start | bytes 5087232 | tf_op jit(solution)/shard_map/reduce_scatter | solution.py:105
  68.4 4.4 copy-start.4
  72.7 5.0 copy-start.5
  72.7 5.0 copy-start.6
  78.0 8.8 %copy-start.11 = (f32[8]{0:T(128)S(1)}, f32[8]{0:T(128)}, u32[]{:S(2)}) copy-start(f32[8]{0:T(128)} %param.19) | copy-start | bytes 100
  86.2 0.6 copy-start.7
  120.0 0.7 copy-start.9
  120.0 36.5 %copy-start.2 = (bf16[96,2880]{1,0:T(8,128)(2,1)S(1)}, bf16[96,2880]{1,0:T(8,128)(2,1)}, u32[]{:S(2)}) copy-start(bf16[96,2880]{1,0:T(8,128)(2,1)} %param.14) | copy-start | bytes 1658884
  120.0 37.8 %copy-start.10 = (f32[2880]{0:T(1024)S(1)}, f32[2880]{0:T(1024)}, u32[]{:S(2)}) copy-start(f32[2880]{0:T(1024)} %param.21) | copy-start | bytes 34564
  410.6 9.0 %copy-start.8 = (bf16[2880,32]{0,1:T(8,128)(2,1)S(1)}, bf16[2880,32]{0,1:T(8,128)(2,1)}, u32[]{:S(2)}) copy-start(bf16[2880,32]{0,1:T(8,128)(2,1)} %param.22) | copy-start | bytes 552964
  410.6 157.0 %all-to-all-start.2 = ((bf16[128,14,2880]{2,1,0:T(8,128)(2,1)}), bf16[128,14,2880]{2,1,0:T(8,128)(2,1)}, u32[]{:S(2)}, u32[]{:S(2)}) async-start(bf16[128,14,2880]{2,1,0:T(8,128)(2,1)} %reshape.424), calls=%async_computation.3 | async-start | bytes 24117248 | tf_op jit(solution)/shard_map/all_to_all | solution.py:143
  592.1 13.1 %copy-start.1 = (bf16[512,2880]{0,1:T(8,128)(2,1)S(1)}, bf16[512,2880]{0,1:T(8,128)(2,1)}, u32[]{:S(2)}) copy-start(bf16[512,2880]{0,1:T(8,128)(2,1)} %param.20) | copy-start | bytes 8847364
  597.6 6.5 %copy-start.3 = (bf16[96,2880]{1,0:T(8,128)(2,1)S(1)}, bf16[96,2880]{1,0:T(8,128)(2,1)}, u32[]{:S(2)}) copy-start(bf16[96,2880]{1,0:T(8,128)(2,1)} %reduce-scatter.2.cloned.1.call-done) | copy-start | bytes 1658884
Sparse Core Ops, SparseCore 0:
  120.2 36.2 reduce-scatter.1
